TPU v7x, 256 devices: a whole 4x4x8 slice. The times are simulated.
256 devices in a mesh: seq: 8 (over z_hi, core), chan: 16 (over y, x), dp: 2 (over z_lo).
Axes of the slice: x: 4, y: 4, z: 8 (z_hi: 4, z_lo: 2; z = z_hi * 2 + z_lo), core: 2. Of those that a mesh axis runs over, the one named last changes fastest.
Arguments:
- query_proj: bfloat16 [2, 4096, 8192], P('dp', 'seq', 'chan'), may hold values from -6 to 6
- key_proj: bfloat16 [2, 4096, 8192], P('dp', 'seq', 'chan')
- value_proj: bfloat16 [2, 4096, 8192], P('dp', 'seq', 'chan')
- cotangent: bfloat16 [2, 4096, 8192], P('dp', 'seq', 'chan'), may hold values from -6 to 6
- long_filter: float32 [4096, 8192], P('seq', 'chan')
- skip_gain: float32 [8192], P('chan'), may hold values from -3 to 3
Outputs:
- output: bfloat16 [2, 4096, 8192], P('dp', 'seq', 'chan')
- grad_query: bfloat16 [2, 4096, 8192], P('dp', 'seq', 'chan')
- grad_key: bfloat16 [2, 4096, 8192], P('dp', 'seq', 'chan')
- grad_value: bfloat16 [2, 4096, 8192], P('dp', 'seq', 'chan')
- grad_filter: float32 [4096, 8192], P('seq', 'chan')
- grad_skip: float32 [8192], P('chan')
All inputs are finite; a program needn't handle non-finite values.
Results may differ from a plain program's by a relative error of at most 0.0095.
Values may be sent and summed in bfloat16 or wider, within the bound.
No kernel may reach another device: no remote copies, remote signals or barrier semaphores. Data moves between devices by JAX's collectives and lax.ppermute only.
A program may use at most 64 MiB of HBM per device.

v0:
```python
import math

import jax
import jax.numpy as jnp
from jax import lax
from jax.sharding import PartitionSpec as P

full_precision = lax.Precision.HIGHEST


def spectral_tables(seq_length):
    full_size = 2 * seq_length
    inner = 128
    outer = full_size // inner
    rows = seq_length // inner
    half = outer // 2 + 1
    k_index = jnp.arange(half, dtype=jnp.int32)
    n_index = jnp.arange(rows, dtype=jnp.int32)
    m_index = jnp.arange(inner, dtype=jnp.int32)
    j_index = jnp.arange(inner, dtype=jnp.int32)
    first_angle = (2.0 * math.pi / outer) * (
        (k_index[:, None] * n_index[None, :]) % outer
    ).astype(jnp.float32)
    first_cos = jnp.cos(first_angle)
    first_sin = jnp.sin(first_angle)
    stage_a = jnp.concatenate([first_cos, -first_sin], axis=0)
    weight = jnp.where((k_index == 0) | (k_index == outer // 2), 1.0, 2.0) / full_size
    inv_a = jnp.concatenate(
        [(first_cos * weight[:, None]).T, (-first_sin * weight[:, None]).T], axis=1
    )
    twist_angle = (2.0 * math.pi / full_size) * (
        (k_index[:, None] * m_index[None, :]) % full_size
    ).astype(jnp.float32)
    twist_cos, twist_sin = jnp.cos(twist_angle), jnp.sin(twist_angle)
    last_angle = (2.0 * math.pi / inner) * (
        (j_index[:, None] * m_index[None, :]) % inner
    ).astype(jnp.float32)
    last_cos, last_sin = jnp.cos(last_angle), jnp.sin(last_angle)
    g_re = twist_cos[:, None, :] * last_cos[None] - twist_sin[:, None, :] * last_sin[None]
    g_im = -(twist_sin[:, None, :] * last_cos[None] + twist_cos[:, None, :] * last_sin[None])
    fwd_table = jnp.concatenate([g_re, g_im], axis=1).astype(jnp.bfloat16)
    g_re_t = jnp.swapaxes(g_re, 1, 2)
    g_im_t = jnp.swapaxes(g_im, 1, 2)
    inv_table = jnp.concatenate([g_re_t, -g_im_t], axis=1).astype(jnp.bfloat16)
    return stage_a, inv_a, fwd_table, inv_table


def complex_stage(table, real_part, imag_part):
    inner = real_part.shape[1]
    a = jnp.einsum(
        "kjm,kml->kjl", table, real_part.astype(jnp.bfloat16),
        preferred_element_type=jnp.float32,
    )
    b = jnp.einsum(
        "kjm,kml->kjl", table, imag_part.astype(jnp.bfloat16),
        preferred_element_type=jnp.float32,
    )
    out_real = a[:, :inner] - b[:, inner:]
    out_imag = b[:, :inner] + a[:, inner:]
    return out_real, out_imag


def forward_spectrum(slab, tables):
    stage_a, _, fwd_table, _ = tables
    half = fwd_table.shape[0]
    first = jnp.einsum("kn,nml->kml", stage_a, slab, precision=full_precision)
    return complex_stage(fwd_table, first[:half], first[half:])


def inverse_spectrum(prod_re, prod_im, tables):
    _, inv_a, _, inv_table = tables
    back_re, back_im = complex_stage(inv_table, prod_re, prod_im)
    both = jnp.concatenate([back_re, back_im], axis=0)
    return jnp.einsum("nk,kml->nml", inv_a, both, precision=full_precision)


def spectral_block(signals, taps):
    seq_length, lanes = signals.shape
    tables = spectral_tables(seq_length)
    inner = tables[2].shape[2]
    rows = seq_length // inner
    half_lanes = lanes // 2
    sig_re, sig_im = forward_spectrum(signals.reshape(rows, inner, lanes), tables)
    taps_re, taps_im = forward_spectrum(taps.reshape(rows, inner, lanes), tables)
    lane = lax.broadcasted_iota(jnp.int32, (1, 1, lanes), 2)
    taps_im = jnp.where(lane < half_lanes, taps_im, -taps_im)
    pair_re = sig_re * taps_re - sig_im * taps_im
    pair_im = sig_re * taps_im + sig_im * taps_re
    turned_re = jnp.roll(sig_re, half_lanes, axis=2)
    turned_im = jnp.roll(sig_im, half_lanes, axis=2)
    cross_re = sig_re * turned_re + sig_im * turned_im
    cross_im = sig_re * turned_im - sig_im * turned_re
    pair = inverse_spectrum(pair_re, pair_im, tables).reshape(seq_length, lanes)
    cross = inverse_spectrum(cross_re, cross_im, tables).reshape(seq_length, lanes)
    return pair, cross


def on_device(query_proj, key_proj, value_proj, cotangent, long_filter, skip_gain):
    query_rows = query_proj[0].astype(jnp.float32)
    key_rows = key_proj[0].astype(jnp.float32)
    value_rows = value_proj[0].astype(jnp.float32)
    cot_rows = cotangent[0].astype(jnp.float32)
    local_length, chan_width = query_proj.shape[1], query_proj.shape[2]
    seq_count = lax.axis_size("seq")
    batch_count = lax.axis_size("dp")
    groups = seq_count * batch_count
    share = chan_width // groups
    seq_length = seq_count * local_length
    factor = (batch_count * seq_length) ** (-0.5)
    mixed = (key_rows * value_rows).astype(jnp.bfloat16)
    weighted = (cot_rows * query_rows).astype(jnp.bfloat16)

    pair = jnp.stack([mixed.T, weighted.T], axis=0).reshape(2, groups, share, local_length)
    pair = jnp.transpose(pair, (1, 0, 2, 3))
    pair_cols = lax.all_to_all(pair, ("seq", "dp"), 0, 0, tiled=True)
    taps_t = long_filter.T.reshape(seq_count, batch_count, share, local_length)
    taps_mine = lax.dynamic_index_in_dim(taps_t, lax.axis_index("dp"), axis=1, keepdims=False)
    taps_cols = lax.all_to_all(taps_mine, "seq", 0, 0, tiled=True)

    mixed_wide = mixed.astype(jnp.float32)
    weighted_wide = weighted.astype(jnp.float32)
    gain_part = jnp.sum(weighted_wide * mixed_wide, axis=0)
    grad_skip = factor * lax.psum(gain_part, ("seq", "dp"))
    grad_skip, pair_cols, taps_cols = lax.optimization_barrier((grad_skip, pair_cols, taps_cols))

    pair_t = pair_cols.reshape(seq_count, batch_count, 2, share, local_length)
    signals = jnp.transpose(pair_t, (0, 4, 2, 1, 3)).reshape(seq_length, 2 * batch_count * share)
    taps = jnp.transpose(taps_cols, (0, 2, 1)).reshape(seq_length, 1, share)
    taps = jnp.broadcast_to(taps, (seq_length, 2 * batch_count, share)).reshape(
        seq_length, 2 * batch_count * share
    )

    pair_vals, cross = spectral_block(signals.astype(jnp.float32), taps)
    pair_vals = pair_vals.reshape(seq_length, 2, batch_count, share)
    cross = cross.reshape(seq_length, 2, batch_count, share)
    slope = jnp.sum(cross[:, 0], axis=1)

    pair_back = pair_vals.astype(jnp.bfloat16).reshape(
        seq_count, local_length, 2, batch_count, share
    )
    pair_back = jnp.transpose(pair_back, (0, 3, 2, 1, 4))
    pair_back = jnp.swapaxes(pair_back, 3, 4).reshape(groups, 2, share, local_length)
    pair_home = lax.all_to_all(pair_back, ("seq", "dp"), 0, 0, tiled=True)
    pair_home = jnp.transpose(pair_home, (1, 0, 2, 3)).reshape(2, chan_width, local_length)
    conv_rows = pair_home[0].T.astype(jnp.float32)
    corr_rows = pair_home[1].T.astype(jnp.float32)

    slope_blocks = jnp.swapaxes(slope.reshape(seq_count, local_length, share), 1, 2)
    slope_send = jnp.broadcast_to(
        slope_blocks[:, None], (seq_count, batch_count, share, local_length)
    ).reshape(groups, share, local_length)
    slope_home = lax.all_to_all(slope_send, ("seq", "dp"), 0, 0, tiled=True)
    grad_filter = factor * slope_home.reshape(chan_width, local_length).T

    signal = conv_rows + skip_gain[None, :] * mixed_wide
    output = (query_rows * signal).astype(jnp.bfloat16)
    grad_query = (cot_rows * signal).astype(jnp.bfloat16)
    back = corr_rows + skip_gain[None, :] * weighted_wide
    grad_key = (back * value_rows).astype(jnp.bfloat16)
    grad_value = (back * key_rows).astype(jnp.bfloat16)
    return (
        output[None],
        grad_query[None],
        grad_key[None],
        grad_value[None],
        grad_filter,
        grad_skip,
    )


def solution(mesh):
    return jax.shard_map(
        on_device,
        mesh=mesh,
        in_specs=(
            P("dp", "seq", "chan"),
            P("dp", "seq", "chan"),
            P("dp", "seq", "chan"),
            P("dp", "seq", "chan"),
            P("seq", "chan"),
            P("chan"),
        ),
        out_specs=(
            P("dp", "seq", "chan"),
            P("dp", "seq", "chan"),
            P("dp", "seq", "chan"),
            P("dp", "seq", "chan"),
            P("seq", "chan"),
            P("chan"),
        ),
        check_vma=False,
    )
```

profile of v0, /device:TPU:1, one launch (start us, length us, event | category | flops | bytes accessed | tf_op | source)
XLA Modules:
  0.0 208.5 jit_solution(18292226019114868031)
XLA Ops:
  0.7 1.6 copy.93
  3.2 10.0 %all-to-all-start.1 = ((f32[8,32,512]{2,1,0:T(8,128)}), f32[8,32,512]{2,1,0:T(8,128)S(1)}, u32[]{:S(2)}, u32[]{:S(2)}) async-start(f32[8,32,512]{2,1,0:T(8,128)} %dynamic-slice_bitcast_fusion), calls=%async_computation.1 | async-start | bytes 1048576 | tf_op jit(solution)/shard_map/all_to_all | solution.py:118
  17.7 9.5 %all-to-all-done.1 = f32[8,32,512]{2,1,0:T(8,128)S(1)} async-done(((f32[8,32,512]{2,1,0:T(8,128)}), f32[8,32,512]{2,1,0:T(8,128)S(1)}, u32[]{:S(2)}, u32[]{:S(2)}) %all-to-all-start.1) | async-done | bytes 524320 | tf_op jit(solution)/shard_map/all_to_all | solution.py:118
  27.3 8.0 %all-to-all-start = ((bf16[16,2,32,512]{3,2,1,0:T(8,128)(2,1)}), bf16[16,2,32,512]{3,2,1,0:T(8,128)(2,1)}, u32[]{:S(2)}, u32[]{:S(2)}) async-start(bf16[16,2,32,512]{3,2,1,0:T(8,128)(2,1)} %copy.92), calls=%async_computation | async-start | bytes 2097152 | tf_op jit(solution)/shard_map/all_to_all | solution.py:115
  35.3 44.4 %psum.7 = f32[512]{0:T(512)S(1)} all-reduce(f32[512]{0:T(512)S(1)} %get-tuple-element.30), channel_id=1, replica_groups=mesh['seq'=8,'chan'=16,'dp'=2] {'seq','dp'}, use_global_device_ids=true, to_apply=%region_1.2 | all-reduce | flops 512 | bytes 4096 | tf_op jit(solution)/shard_map/psum | solution.py:123
  80.9 2.8 %subtract_convert_fusion.3 = (bf16[33,128,128]{2,1,0:T(8,128)(2,1)S(1)}, bf16[33,128,128]{2,1,0:T(8,128)(2,1)}, bf16[33,128,128]{2,1,0:T(8,128)(2,1)S(1)}, bf16[33,128,128]{2,1,0:T(8,128)(2,1)S(1)}) fusion(f32[128,128]{1,0:T(8,128)S(1)} %get-tuple-element.63, f32[33,128]{1,0:T(8,128)S(1)} %get-tuple-element.65, f32[128,128]{1,0:T(8,128)S(1)} %get-tuple-element.64, ...), kind=kLoop, calls=%fused_computation.24 | loop fusion | flops 9191424 | bytes 4490240 | tf_op jit(solution)/shard_map/convert.14
  83.7 2.8 %copy.146 = bf16[8,2,2,32,512]{4,0,3,1,2:T(8,128)(2,1)} copy(bf16[8,2,2,32,512]{4,3,2,1,0:T(8,128)(2,1)} %bitcast.15) | data formatting | bytes 2097152 | tf_op jit(solution)/shard_map/reshape | solution.py:126
  86.4 2.5 %reshape.150 = bf16[32,128,128]{1,0,2:T(8,128)(2,1)} reshape(bf16[8,512,2,2,32]{1,0,4,3,2:T(8,128)(2,1)} %bitcast.127) | data formatting | bytes 2097152 | tf_op jit(solution)/shard_map/reshape | solution.py:83
  88.9 3.2 %copy.95 = bf16[32,128,128]{2,0,1:T(8,128)(2,1)} copy(bf16[32,128,128]{1,0,2:T(8,128)(2,1)} %reshape.150) | data formatting | bytes 2097152 | tf_op jit(solution)/shard_map/reshape | solution.py:83
  92.1 3.3 %convolution_convert_fusion.1 = bf16[66,128,128]{2,0,1:T(8,128)(2,1)S(1)} fusion(bf16[32,128,128]{2,0,1:T(8,128)(2,1)} %copy.95, f32[33,32]{0,1:T(8,128)S(1)} %get-tuple-element.61, f32[33,32]{0,1:T(8,128)S(1)} %get-tuple-element.62), kind=kOutput, calls=%fused_computation.26 | convolution fusion | flops 416319552 | bytes 3219712 | tf_op jit(solution)/shard_map/kn,nml->kml/dot_general | solution.py:66
  96.1 2.8 %fusion.13 = f32[33,256,128]{1,2,0:T(8,128)} fusion(bf16[33,128,128]{2,0,1:T(8,128)(2,1)S(1)} %get-tuple-element.41, bf16[33,128,128]{2,1,0:T(8,128)(2,1)S(1)} %get-tuple-element.56, bf16[33,128,128]{2,1,0:T(8,128)(2,1)S(1)} %get-tuple-element.55), kind=kOutput, calls=%fused_computation.45 | convolution fusion | flops 281149440 | bytes 7569408 | tf_op jit(solution)/shard_map/kjm,kml->kjl/dot_general | solution.py:54
  98.9 2.8 %fusion.15 = f32[33,256,128]{1,2,0:T(8,128)} fusion(bf16[33,128,128]{2,0,1:T(8,128)(2,1)S(1)} %get-tuple-element.42, bf16[33,128,128]{2,1,0:T(8,128)(2,1)S(1)} %get-tuple-element.56, bf16[33,128,128]{2,1,0:T(8,128)(2,1)S(1)} %get-tuple-element.55), kind=kOutput, calls=%fused_computation.47 | convolution fusion | flops 281149440 | bytes 7569408 | tf_op jit(solution)/shard_map/kjm,kml->kjl/dot_general | solution.py:50
  102.0 1.7 copy.131
  103.6 3.4 %copy.99 = f32[32,128,128]{2,0,1:T(8,128)} copy(f32[32,128,128]{1,0,2:T(8,128)} %bitcast.122) | data formatting | bytes 4194304 | tf_op jit(solution)/shard_map/reshape;reshape | solution.py:84
  107.1 5.5 %convolution_convert_fusion = bf16[66,128,128]{2,0,1:T(8,128)(2,1)S(1)} fusion(f32[32,128,128]{2,0,1:T(8,128)} %copy.99, f32[33,32]{0,1:T(8,128)S(1)} %get-tuple-element.61, f32[33,32]{0,1:T(8,128)S(1)} %get-tuple-element.62), kind=kOutput, calls=%fused_computation.25 | convolution fusion | flops 416319552 | bytes 4268288 | tf_op jit(solution)/shard_map/kn,nml->kml/dot_general | solution.py:66
  121.3 1.5 fusion.71
  124.0 6.2 %fusion.2 = bf16[32,128,128]{2,0,1:T(8,128)(2,1)} fusion(f32[66,128,128]{2,1,0:T(8,128)S(1)} %pad_maximum_fusion, f32[32,33]{1,0:T(8,128)S(1)} %get-tuple-element.60, f32[32,33]{1,0:T(8,128)S(1)} %get-tuple-element.59), kind=kOutput, calls=%fused_computation.27 | convolution fusion | flops 415762496 | bytes 5382400 | tf_op jit(solution)/shard_map/nk,kml->nml/dot_general | solution.py:74
  130.1 3.3 %copy.109 = bf16[32,128,128]{1,0,2:T(8,128)(2,1)} copy(bf16[32,128,128]{2,0,1:T(8,128)(2,1)} %fusion.2) | data formatting | bytes 2097152 | tf_op jit(solution)/shard_map/convert_element_type | solution.py:138
  133.4 2.5 %convert_element_type.156 = bf16[8,512,2,2,32]{1,0,4,3,2:T(8,128)(2,1)} reshape(bf16[32,128,128]{1,0,2:T(8,128)(2,1)} %copy.109) | data formatting | bytes 2097152 | tf_op jit(solution)/shard_map/convert_element_type | solution.py:138
  135.8 2.5 %copy.110 = bf16[8,2,2,32,512]{4,3,2,1,0:T(8,128)(2,1)} copy(bf16[8,2,2,32,512]{4,0,3,1,2:T(8,128)(2,1)} %bitcast.128) | data formatting | bytes 2097152 | tf_op jit(solution)/shard_map/transpose;transpose | solution.py:142
  138.4 7.3 %all-to-all-start.2 = ((bf16[16,2,32,512]{3,2,1,0:T(8,128)(2,1)}), bf16[16,2,32,512]{3,2,1,0:T(8,128)(2,1)}, u32[]{:S(2)}, u32[]{:S(2)}) async-start(bf16[16,2,32,512]{3,2,1,0:T(8,128)(2,1)} %bitcast.125), calls=%async_computation.2 | async-start | bytes 2097152 | tf_op jit(solution)/shard_map/all_to_all | solution.py:143
  145.7 4.1 %fusion.8 = f32[33,256,128]{2,1,0:T(8,128)S(1)} fusion(f32[33,128,128]{1,2,0:T(8,128)} %copy-done, f32[33,128,128]{1,2,0:T(8,128)S(1)} %get-tuple-element.37, f32[33,128,64]{1,2,0:T(8,128)} %get-tuple-element.46, f32[33,128,64]{1,2,0:T(8,128)} %get-tuple-element.45, f32[33,128,64]{1,2,0:T(8,128)} %get-tuple-element.44, ...), kind=kOutput, calls=%fused_computation.40 | convolution fusion | flops 284393472 | bytes 15138816 | tf_op jit(solution)/shard_map/kjm,kml->kjl/dot_general | solution.py:54
  153.1 2.6 %pad_maximum_fusion.1 = f32[66,128,128]{2,1,0:T(8,128)} fusion(f32[33,128,128]{2,1,0:T(8,128)S(1)} %get-tuple-element.34, f32[33,128,128]{2,1,0:T(8,128)S(1)} %get-tuple-element.33), kind=kLoop, calls=%fused_computation.3 | loop fusion | flops 1081344 | bytes 8650752 | tf_op jit(solution)/shard_map/concatenate | solution.py:73
  155.7 5.7 %copy.127 = f32[66,128,128]{1,0,2:T(8,128)} copy(f32[66,128,128]{2,1,0:T(8,128)} %pad_maximum_fusion.1) | data formatting | bytes 8650752 | tf_op jit(solution)/shard_map/concatenate | solution.py:73
  161.4 4.3 %fusion.59 = f32[32,128,128]{1,0,2:T(8,128)S(1)} fusion(f32[66,128,128]{1,0,2:T(8,128)} %copy.127, f32[32,33]{1,0:T(8,128)S(1)} %get-tuple-element.60, f32[32,33]{1,0:T(8,128)S(1)} %get-tuple-element.59), kind=kOutput, calls=%fused_computation.115 | convolution fusion | flops 415238208 | bytes 6430976 | tf_op jit(solution)/shard_map/nk,kml->nml/dot_general | solution.py:74
  165.7 1.6 reshape_reshape.8
  169.2 3.5 %all-to-all-done.2 = bf16[16,2,32,512]{3,2,1,0:T(8,128)(2,1)} async-done(((bf16[16,2,32,512]{3,2,1,0:T(8,128)(2,1)}), bf16[16,2,32,512]{3,2,1,0:T(8,128)(2,1)}, u32[]{:S(2)}, u32[]{:S(2)}) %all-to-all-start.2) | async-done | bytes 1048608 | tf_op jit(solution)/shard_map/all_to_all | solution.py:143
  173.9 4.7 %all-to-all-start.3 = ((f32[16,32,512]{2,1,0:T(8,128)}), f32[16,32,512]{2,1,0:T(8,128)}, u32[]{:S(2)}, u32[]{:S(2)}) async-start(f32[16,32,512]{2,1,0:T(8,128)} %bitcast.126), calls=%async_computation.3 | async-start | bytes 2097152 | tf_op jit(solution)/shard_map/all_to_all | solution.py:152
  180.0 2.0 fusion.26
  182.0 2.1 %copy.116 = bf16[1,512,512]{2,1,0:T(8,128)(2,1)} copy(bf16[1,512,512]{1,2,0:T(8,128)(2,1)} %get-tuple-element.57) | data formatting | bytes 1048576
  184.2 2.0 copy.117
  188.2 17.5 %all-to-all-done.3 = f32[16,32,512]{2,1,0:T(8,128)} async-done(((f32[16,32,512]{2,1,0:T(8,128)}), f32[16,32,512]{2,1,0:T(8,128)}, u32[]{:S(2)}, u32[]{:S(2)}) %all-to-all-start.3) | async-done | bytes 1048608 | tf_op jit(solution)/shard_map/all_to_all | solution.py:152
  (105 shorter events, 29.4 us)
Async XLA Ops:
  0.6 12.5 %copy-start.24 = (bf16[1,512,512]{2,1,0:T(8,128)(2,1)S(1)}, bf16[1,512,512]{2,1,0:T(8,128)(2,1)}, u32[]{:S(2)}) copy-start(bf16[1,512,512]{2,1,0:T(8,128)(2,1)} %param.6) | copy-start | bytes 1572868
  0.6 12.7 %copy-start.25 = (bf16[1,512,512]{2,1,0:T(8,128)(2,1)S(1)}, bf16[1,512,512]{2,1,0:T(8,128)(2,1)}, u32[]{:S(2)}) copy-start(bf16[1,512,512]{2,1,0:T(8,128)(2,1)} %param.9) | copy-start | bytes 1572868
  2.3 11.3 %copy-start.26 = (bf16[1,512,512]{2,1,0:T(8,128)(2,1)S(1)}, bf16[1,512,512]{2,1,0:T(8,128)(2,1)}, u32[]{:S(2)}) copy-start(bf16[1,512,512]{2,1,0:T(8,128)(2,1)} %param.8) | copy-start | bytes 1572868
  3.2 24.1 %all-to-all-start.1 = ((f32[8,32,512]{2,1,0:T(8,128)}), f32[8,32,512]{2,1,0:T(8,128)S(1)}, u32[]{:S(2)}, u32[]{:S(2)}) async-start(f32[8,32,512]{2,1,0:T(8,128)} %dynamic-slice_bitcast_fusion), calls=%async_computation.1 | async-start | bytes 1048576 | tf_op jit(solution)/shard_map/all_to_all | solution.py:118
  13.4 2.3 %copy-start.8 = (bf16[1,512,512]{1,2,0:T(8,128)(2,1)}, bf16[1,512,512]{1,2,0:T(8,128)(2,1)S(1)}, u32[]{:S(2)}) copy-start(bf16[1,512,512]{1,2,0:T(8,128)(2,1)S(1)} %copy.88) | copy-start | bytes 1572868
  13.6 2.1 %copy-start.10 = (bf16[1,512,512]{1,2,0:T(8,128)(2,1)}, bf16[1,512,512]{1,2,0:T(8,128)(2,1)S(1)}, u32[]{:S(2)}) copy-start(bf16[1,512,512]{1,2,0:T(8,128)(2,1)S(1)} %copy.89) | copy-start | bytes 1572868
  13.8 2.8 %copy-start.12 = (bf16[1,512,512]{1,2,0:T(8,128)(2,1)}, bf16[1,512,512]{1,2,0:T(8,128)(2,1)S(1)}, u32[]{:S(2)}) copy-start(bf16[1,512,512]{1,2,0:T(8,128)(2,1)S(1)} %copy.91) | copy-start | bytes 1572868
  27.3 53.6 %copy-start.22 = (f32[8,32,512]{2,1,0:T(8,128)}, f32[8,32,512]{2,1,0:T(8,128)S(1)}, u32[]{:S(2)}) copy-start(f32[8,32,512]{2,1,0:T(8,128)S(1)} %all-to-all-done.1) | copy-start | bytes 1572868
  27.3 56.4 %all-to-all-start = ((bf16[16,2,32,512]{3,2,1,0:T(8,128)(2,1)}), bf16[16,2,32,512]{3,2,1,0:T(8,128)(2,1)}, u32[]{:S(2)}, u32[]{:S(2)}) async-start(bf16[16,2,32,512]{3,2,1,0:T(8,128)(2,1)} %copy.92), calls=%async_computation | async-start | bytes 2097152 | tf_op jit(solution)/shard_map/all_to_all | solution.py:115
  98.9 2.8 %copy-start.23 = (f32[8,32,512]{2,1,0:T(8,128)S(1)}, f32[8,32,512]{2,1,0:T(8,128)}, u32[]{:S(2)}) copy-start(f32[8,32,512]{2,1,0:T(8,128)} %copy-done.22) | copy-start | bytes 1572868
  112.6 2.3 %slice-start.2 = ((s8[4325376]{0:T(1024)(128)(4,1)}), s8[4194304]{0:T(1024)(128)(4,1)S(1)}, s32[]{:S(2)}) async-start(s8[4325376]{0:T(1024)(128)(4,1)} %bitcast.119), calls=%async_computation.6 | async-start | bytes 8388608
  113.3 3.0 %slice-start = ((s8[4325376]{0:T(1024)(128)(4,1)}), s8[4194304]{0:T(1024)(128)(4,1)S(1)}, s32[]{:S(2)}) async-start(s8[4325376]{0:T(1024)(128)(4,1)} %bitcast.117), calls=%async_computation.4 | async-start | bytes 8388608
  113.3 3.0 %slice-start.3 = ((s8[4325376]{0:T(1024)(128)(4,1)}), s8[131072]{0:T(1024)(128)(4,1)S(1)}, s32[]{:S(2)}) async-start(s8[4325376]{0:T(1024)(128)(4,1)} %bitcast.119), calls=%async_computation.7 | async-start | bytes 262144
  114.1 2.2 %slice-start.1 = ((s8[4325376]{0:T(1024)(128)(4,1)}), s8[131072]{0:T(1024)(128)(4,1)S(1)}, s32[]{:S(2)}) async-start(s8[4325376]{0:T(1024)(128)(4,1)} %bitcast.117), calls=%async_computation.5 | async-start | bytes 262144
  116.8 3.0 %copy-start = (f32[33,128,128]{1,2,0:T(8,128)}, f32[33,128,128]{1,2,0:T(8,128)S(1)}, u32[]{:S(2)}) copy-start(f32[33,128,128]{1,2,0:T(8,128)S(1)} %get-tuple-element.38) | copy-start | bytes 6488068
  138.4 34.4 %all-to-all-start.2 = ((bf16[16,2,32,512]{3,2,1,0:T(8,128)(2,1)}), bf16[16,2,32,512]{3,2,1,0:T(8,128)(2,1)}, u32[]{:S(2)}, u32[]{:S(2)}) async-start(bf16[16,2,32,512]{3,2,1,0:T(8,128)(2,1)} %bitcast.125), calls=%async_computation.2 | async-start | bytes 2097152 | tf_op jit(solution)/shard_map/all_to_all | solution.py:143
  145.7 4.2 %copy-start.1 = (f32[33,128,128]{1,2,0:T(8,128)S(1)}, f32[33,128,128]{1,2,0:T(8,128)}, u32[]{:S(2)}) copy-start(f32[33,128,128]{1,2,0:T(8,128)} %copy-done) | copy-start | bytes 6488068
  145.7 4.2 %copy-start.3 = (bf16[33,128,128]{2,1,0:T(8,128)(2,1)S(1)}, bf16[33,128,128]{2,1,0:T(8,128)(2,1)}, u32[]{:S(2)}) copy-start(bf16[33,128,128]{2,1,0:T(8,128)(2,1)} %get-tuple-element.54) | copy-start | bytes 3244036
  145.7 4.4 %copy-start.4 = (f32[33,128,64]{1,2,0:T(8,128)S(1)}, f32[33,128,64]{1,2,0:T(8,128)}, u32[]{:S(2)}) copy-start(f32[33,128,64]{1,2,0:T(8,128)} %get-tuple-element.45) | copy-start | bytes 3244036
  145.7 4.7 %copy-start.5 = (f32[33,128,64]{1,2,0:T(8,128)S(1)}, f32[33,128,64]{1,2,0:T(8,128)}, u32[]{:S(2)}) copy-start(f32[33,128,64]{1,2,0:T(8,128)} %get-tuple-element.46) | copy-start | bytes 3244036
  145.7 5.1 %copy-start.6 = (f32[33,128,64]{1,2,0:T(8,128)S(1)}, f32[33,128,64]{1,2,0:T(8,128)}, u32[]{:S(2)}) copy-start(f32[33,128,64]{1,2,0:T(8,128)} %get-tuple-element.43) | copy-start | bytes 3244036
  145.7 5.4 %copy-start.7 = (f32[33,128,64]{1,2,0:T(8,128)S(1)}, f32[33,128,64]{1,2,0:T(8,128)}, u32[]{:S(2)}) copy-start(f32[33,128,64]{1,2,0:T(8,128)} %get-tuple-element.44) | copy-start | bytes 3244036
  173.9 6.1 %copy-start.9 = (bf16[1,512,512]{1,2,0:T(8,128)(2,1)S(1)}, bf16[1,512,512]{1,2,0:T(8,128)(2,1)}, u32[]{:S(2)}) copy-start(bf16[1,512,512]{1,2,0:T(8,128)(2,1)} %copy-done.8) | copy-start | bytes 1572868
  173.9 6.1 %copy-start.11 = (bf16[1,512,512]{1,2,0:T(8,128)(2,1)S(1)}, bf16[1,512,512]{1,2,0:T(8,128)(2,1)}, u32[]{:S(2)}) copy-start(bf16[1,512,512]{1,2,0:T(8,128)(2,1)} %copy-done.10) | copy-start | bytes 1572868
  173.9 6.1 %copy-start.13 = (bf16[1,512,512]{1,2,0:T(8,128)(2,1)S(1)}, bf16[1,512,512]{1,2,0:T(8,128)(2,1)}, u32[]{:S(2)}) copy-start(bf16[1,512,512]{1,2,0:T(8,128)(2,1)} %copy-done.12) | copy-start | bytes 1572868
  173.9 6.1 %copy-start.15 = (bf16[1,512,512]{1,2,0:T(8,128)(2,1)S(1)}, bf16[1,512,512]{1,2,0:T(8,128)(2,1)}, u32[]{:S(2)}) copy-start(bf16[1,512,512]{1,2,0:T(8,128)(2,1)} %copy-done.14) | copy-start | bytes 1572868
  173.9 6.1 %copy-start.17 = (bf16[512,512]{0,1:T(8,128)(2,1)S(1)}, bf16[512,512]{0,1:T(8,128)(2,1)}, u32[]{:S(2)}) copy-start(bf16[512,512]{0,1:T(8,128)(2,1)} %copy-done.16) | copy-start | bytes 1572868
  173.9 6.1 %copy-start.19 = (bf16[512,512]{0,1:T(8,128)(2,1)S(1)}, bf16[512,512]{0,1:T(8,128)(2,1)}, u32[]{:S(2)}) copy-start(bf16[512,512]{0,1:T(8,128)(2,1)} %copy-done.18) | copy-start | bytes 1572868
  173.9 6.1 %copy-start.27 = (f32[512]{0:T(512)S(1)}, f32[512]{0:T(512)}, u32[]{:S(2)}) copy-start(f32[512]{0:T(512)} %param.11) | copy-start | bytes 6148
  173.9 31.8 %all-to-all-start.3 = ((f32[16,32,512]{2,1,0:T(8,128)}), f32[16,32,512]{2,1,0:T(8,128)}, u32[]{:S(2)}, u32[]{:S(2)}) async-start(f32[16,32,512]{2,1,0:T(8,128)} %bitcast.126), calls=%async_computation.3 | async-start | bytes 2097152 | tf_op jit(solution)/shard_map/all_to_all | solution.py:152
  182.0 4.2 %copy-start.21 = (bf16[1,512,512]{1,2,0:T(8,128)(2,1)S(1)}, bf16[1,512,512]{1,2,0:T(8,128)(2,1)}, u32[]{:S(2)}) copy-start(bf16[1,512,512]{1,2,0:T(8,128)(2,1)} %get-tuple-element.48) | copy-start | bytes 1572868
  182.0 5.2 %copy-start.20 = (bf16[1,512,512]{1,2,0:T(8,128)(2,1)S(1)}, bf16[1,512,512]{1,2,0:T(8,128)(2,1)}, u32[]{:S(2)}) copy-start(bf16[1,512,512]{1,2,0:T(8,128)(2,1)} %get-tuple-element.47) | copy-start | bytes 1572868
  (4 other events, 4.3 us)
where the time goes:
time: 209 us; the launch traced here: 208 us
  local copies, waits for them, and re-layouts  53.9 us (26%)
  blocking collectives  44.4 us (21%)
  matrix products  33.8 us (16%)
  waiting for transfers between devices  30.6 us (15%)
  starting transfers between devices  30.1 us (14%)
  other arithmetic  14.5 us (7%)
    psum x1, blocking collectives, on_device(): grad_skip = factor * lax.psum(gain_part, ('seq', 'dp'))  44.4 us
    all_to_all x1, waiting for transfers between devices, on_device(): slope_home = lax.all_to_all(slope_send, ('seq', 'dp'), 0, 0, tiled=True)  17.5 us
    unnamed x76, local copies, waits for them, and re-layouts  17.4 us
    dot_general x2, matrix products, inverse_spectrum(): return jnp.einsum('nk,kml->nml', inv_a, both, precision=full_precision)  10.4 us
    all_to_all x1, starting transfers between devices, on_device(): taps_cols = lax.all_to_all(taps_mine, 'seq', 0, 0, tiled=True)  9.97 us
    all_to_all x1, waiting for transfers between devices, on_device(): taps_cols = lax.all_to_all(taps_mine, 'seq', 0, 0, tiled=True)  9.55 us
    dot_general x2, matrix products, forward_spectrum(): first = jnp.einsum('kn,nml->kml', stage_a, slab, precision=full_precision)  8.88 us
    dot_general x4, matrix products, complex_stage(): jnp.einsum('kjm,kml->kjl', table, imag_part.astype(jnp.bfloat16), preferr...  8.84 us
  transfers between devices with their start and end apart: 4, of which 3 were waited for; matrix products, arithmetic and copies ran while one was open for 19% of the time, Pallas kernels for 0%

commit v1 on v0

--- a/solution.py
+++ b/solution.py
@@ -110,27 +110,31 @@
     mixed = (key_rows * value_rows).astype(jnp.bfloat16)
     weighted = (cot_rows * query_rows).astype(jnp.bfloat16)
 
-    pair = jnp.stack([mixed.T, weighted.T], axis=0).reshape(2, groups, share, local_length)
-    pair = jnp.transpose(pair, (1, 0, 2, 3))
-    pair_cols = lax.all_to_all(pair, ("seq", "dp"), 0, 0, tiled=True)
-    taps_t = long_filter.T.reshape(seq_count, batch_count, share, local_length)
-    taps_mine = lax.dynamic_index_in_dim(taps_t, lax.axis_index("dp"), axis=1, keepdims=False)
-    taps_cols = lax.all_to_all(taps_mine, "seq", 0, 0, tiled=True)
-
     mixed_wide = mixed.astype(jnp.float32)
     weighted_wide = weighted.astype(jnp.float32)
     gain_part = jnp.sum(weighted_wide * mixed_wide, axis=0)
     grad_skip = factor * lax.psum(gain_part, ("seq", "dp"))
-    grad_skip, pair_cols, taps_cols = lax.optimization_barrier((grad_skip, pair_cols, taps_cols))
 
-    pair_t = pair_cols.reshape(seq_count, batch_count, 2, share, local_length)
+    pair = jnp.stack([mixed.T, weighted.T], axis=0).reshape(2, groups, share, local_length)
+    pair = jnp.transpose(pair, (1, 0, 2, 3)).reshape(groups, 2 * share, local_length)
+    half_length = local_length // batch_count
+    taps_t = long_filter.T.reshape(groups, share, batch_count, half_length)
+    taps_mine = lax.dynamic_index_in_dim(taps_t, lax.axis_index("dp"), axis=2, keepdims=False)
+    taps_rows = share * half_length // local_length
+    taps_mine = taps_mine.astype(jnp.bfloat16).reshape(groups, taps_rows, local_length)
+    send = jnp.concatenate([pair, taps_mine], axis=1)
+    grad_skip, send = lax.optimization_barrier((grad_skip, send))
+    got = lax.all_to_all(send, ("seq", "dp"), 0, 0, tiled=True)
+
+    pair_t = got[:, : 2 * share].reshape(seq_count, batch_count, 2, share, local_length)
     signals = jnp.transpose(pair_t, (0, 4, 2, 1, 3)).reshape(seq_length, 2 * batch_count * share)
-    taps = jnp.transpose(taps_cols, (0, 2, 1)).reshape(seq_length, 1, share)
+    taps_t = got[:, 2 * share :].reshape(seq_count, batch_count, share, half_length)
+    taps = jnp.transpose(taps_t, (0, 1, 3, 2)).reshape(seq_length, 1, share)
     taps = jnp.broadcast_to(taps, (seq_length, 2 * batch_count, share)).reshape(
         seq_length, 2 * batch_count * share
     )
 
-    pair_vals, cross = spectral_block(signals.astype(jnp.float32), taps)
+    pair_vals, cross = spectral_block(signals.astype(jnp.float32), taps.astype(jnp.float32))
     pair_vals = pair_vals.reshape(seq_length, 2, batch_count, share)
     cross = cross.reshape(seq_length, 2, batch_count, share)
     slope = jnp.sum(cross[:, 0], axis=1)
@@ -138,19 +142,22 @@
     pair_back = pair_vals.astype(jnp.bfloat16).reshape(
         seq_count, local_length, 2, batch_count, share
     )
-    pair_back = jnp.transpose(pair_back, (0, 3, 2, 1, 4))
-    pair_back = jnp.swapaxes(pair_back, 3, 4).reshape(groups, 2, share, local_length)
-    pair_home = lax.all_to_all(pair_back, ("seq", "dp"), 0, 0, tiled=True)
+    pair_back = jnp.transpose(pair_back, (0, 3, 2, 4, 1)).reshape(
+        groups, 2 * share, local_length
+    )
+    slope_blocks = jnp.swapaxes(slope.astype(jnp.bfloat16).reshape(seq_count, local_length, share), 1, 2)
+    slope_send = jnp.broadcast_to(
+        slope_blocks[:, None], (seq_count, batch_count, share, local_length)
+    ).reshape(groups, share, local_length)
+    home = lax.all_to_all(
+        jnp.concatenate([pair_back, slope_send], axis=1), ("seq", "dp"), 0, 0, tiled=True
+    )
+    pair_home = home[:, : 2 * share].reshape(groups, 2, share, local_length)
     pair_home = jnp.transpose(pair_home, (1, 0, 2, 3)).reshape(2, chan_width, local_length)
     conv_rows = pair_home[0].T.astype(jnp.float32)
     corr_rows = pair_home[1].T.astype(jnp.float32)
-
-    slope_blocks = jnp.swapaxes(slope.reshape(seq_count, local_length, share), 1, 2)
-    slope_send = jnp.broadcast_to(
-        slope_blocks[:, None], (seq_count, batch_count, share, local_length)
-    ).reshape(groups, share, local_length)
-    slope_home = lax.all_to_all(slope_send, ("seq", "dp"), 0, 0, tiled=True)
-    grad_filter = factor * slope_home.reshape(chan_width, local_length).T
+    slope_home = home[:, 2 * share :].reshape(chan_width, local_length)
+    grad_filter = factor * slope_home.T.astype(jnp.float32)
 
     signal = conv_rows + skip_gain[None, :] * mixed_wide
     output = (query_rows * signal).astype(jnp.bfloat16)

time: 209 us -> 204 us (0.976)
  blocking collectives: 44.4 us -> 71.8 us
  starting transfers between devices: 30.1 us -> 4.97 us
  local copies, waits for them, and re-layouts: 53.9 us -> 46.7 us
  other arithmetic: 14.5 us -> 17.9 us
  matrix products: 33.8 us -> 31.3 us
    all_to_all x0 -> x1, blocking collectives: none -> 42.2 us  [on_device(): lax.all_to_all(jnp.concatenate([pair_back, slope_send], axis=1), ('seq',...]
    all_to_all x4 -> x1, starting transfers between devices: 30.1 us -> 4.97 us  [on_device(): got = lax.all_to_all(send, ('seq', 'dp'), 0, 0, tiled=True)]
    psum x1, blocking collectives: 44.4 us -> 29.6 us  [on_device(): grad_skip = factor * lax.psum(gain_part, ('seq', 'dp'))]
    another operation x2 -> x0, local copies, waits for them, and re-layouts: 5.94 us -> none  [the longest x1 3.41 us: spectral_block(): taps.reshape(rows, inner, lanes)]
    reshape x1 -> x5, local copies, waits for them, and re-layouts: 2.78 us -> 7.61 us  [the longest x1 3.2 us: spectral_block(): taps.reshape(rows, inner, lanes)]
    convert_element_type x2, local copies, waits for them, and re-layouts: 5.73 us -> 2.2 us  [on_device(): pair_vals.astype(jnp.bfloat16)]
    sub x3, other arithmetic: 2.5 us -> 5.91 us  [complex_stage(): out_real = a[:, :inner] - b[:, inner:]]
    slice x0 -> x3, local copies, waits for them, and re-layouts: none -> 2.37 us  [the longest x1 1.32 us: on_device(): got[:, :2 * share].reshape(seq_count, batch_count, 2, share, local_length)]
  transfers between devices with their start and end apart: 4 -> 1, of which waited for: 3 -> 1; matrix products, arithmetic and copies ran while one was open for 19% -> 2% of each run, Pallas kernels for 0% -> 0%
where the time goes in v1:
time: 204 us; the launch traced here: 203 us
  blocking collectives  71.8 us (35%)
  local copies, waits for them, and re-layouts  46.7 us (23%)
  matrix products  31.3 us (15%)
  waiting for transfers between devices  29 us (14%)
  other arithmetic  17.9 us (9%)
  starting transfers between devices  4.97 us (2%)
    all_to_all x1, blocking collectives, on_device(): lax.all_to_all(jnp.concatenate([pair_back, slope_send], axis=1), ('seq',...  42.2 us
    psum x1, blocking collectives, on_device(): grad_skip = factor * lax.psum(gain_part, ('seq', 'dp'))  29.6 us
    all_to_all x1, waiting for transfers between devices, on_device(): got = lax.all_to_all(send, ('seq', 'dp'), 0, 0, tiled=True)  29 us
    unnamed x61, local copies, waits for them, and re-layouts  16.3 us
    dot_general x2, matrix products, inverse_spectrum(): return jnp.einsum('nk,kml->nml', inv_a, both, precision=full_precision)  9.49 us
    dot_general x4, matrix products, complex_stage(): jnp.einsum('kjm,kml->kjl', table, imag_part.astype(jnp.bfloat16), preferr...  7.58 us
    dot_general x4, matrix products, complex_stage(): jnp.einsum('kjm,kml->kjl', table, real_part.astype(jnp.bfloat16), preferr...  7.57 us
    dot_general x2, matrix products, forward_spectrum(): first = jnp.einsum('kn,nml->kml', stage_a, slab, precision=full_precision)  6.68 us
  transfers between devices with their start and end apart: 1, of which 1 were waited for; matrix products, arithmetic and copies ran while one was open for 2% of the time, Pallas kernels for 0%

profile of v1, /device:TPU:1, one launch (start us, length us, event | category | flops | bytes accessed | tf_op | source)
XLA Modules:
  0.0 202.9 jit_solution(14033071469486658023)
XLA Ops:
  0.7 1.3 copy.27
  2.0 1.4 copy.28
  6.3 1.5 convert_reduce_fusion
  7.9 29.6 %psum.7 = f32[512]{0:T(512)S(1)} all-reduce(f32[512]{0:T(512)S(1)} %get-tuple-element.16), channel_id=1, replica_groups=mesh['seq'=8,'chan'=16,'dp'=2] {'seq','dp'}, use_global_device_ids=true, to_apply=%region_1.0 | all-reduce | flops 512 | bytes 4096 | tf_op jit(solution)/shard_map/psum | solution.py:116
  39.3 5.0 %all-to-all-start = ((bf16[16,80,512]{2,1,0:T(8,128)(2,1)}), bf16[16,80,512]{2,1,0:T(8,128)(2,1)}, u32[]{:S(2)}, u32[]{:S(2)}) async-start(bf16[16,80,512]{2,1,0:T(8,128)(2,1)} %pad_maximum_fusion.7), calls=%async_computation | async-start | bytes 2621440 | tf_op jit(solution)/shard_map/all_to_all | solution.py:127
  45.4 2.8 %subtract_convert_fusion.3 = (bf16[33,128,128]{2,1,0:T(8,128)(2,1)S(1)}, bf16[33,128,128]{2,1,0:T(8,128)(2,1)S(1)}, bf16[33,128,128]{2,1,0:T(8,128)(2,1)S(1)}, bf16[33,128,128]{2,1,0:T(8,128)(2,1)}) fusion(f32[128,128]{1,0:T(8,128)S(1)} %get-tuple-element.49, f32[33,128]{1,0:T(8,128)S(1)} %get-tuple-element.51, f32[128,128]{1,0:T(8,128)S(1)} %get-tuple-element.50, ...), kind=kLoop, calls=%fused_computation.24 | loop fusion | flops 9191424 | bytes 4490240 | tf_op jit(solution)/shard_map/convert.14
  48.1 29.0 %all-to-all-done = bf16[16,80,512]{2,1,0:T(8,128)(2,1)} async-done(((bf16[16,80,512]{2,1,0:T(8,128)(2,1)}), bf16[16,80,512]{2,1,0:T(8,128)(2,1)}, u32[]{:S(2)}, u32[]{:S(2)}) %all-to-all-start) | async-done | bytes 1310752 | tf_op jit(solution)/shard_map/all_to_all | solution.py:127
  77.1 1.3 slice.132
  78.4 1.6 copy.85
  80.0 2.5 %reshape.169 = bf16[32,128,128]{1,0,2:T(8,128)(2,1)} reshape(bf16[8,512,2,2,32]{1,0,4,3,2:T(8,128)(2,1)} %bitcast.128) | data formatting | bytes 2097152 | tf_op jit(solution)/shard_map/reshape | solution.py:83
  82.5 3.2 %copy.34 = bf16[32,128,128]{2,0,1:T(8,128)(2,1)} copy(bf16[32,128,128]{1,0,2:T(8,128)(2,1)} %reshape.169) | data formatting | bytes 2097152 | tf_op jit(solution)/shard_map/reshape | solution.py:83
  85.7 3.3 %convolution_convert_fusion.1 = bf16[66,128,128]{2,0,1:T(8,128)(2,1)S(1)} fusion(bf16[32,128,128]{2,0,1:T(8,128)(2,1)} %copy.34, f32[33,32]{0,1:T(8,128)S(1)} %get-tuple-element.47, f32[33,32]{0,1:T(8,128)S(1)} %get-tuple-element.48), kind=kOutput, calls=%fused_computation.26 | convolution fusion | flops 416319552 | bytes 3219712 | tf_op jit(solution)/shard_map/kn,nml->kml/dot_general | solution.py:66
  90.2 2.8 %fusion.15 = f32[33,256,128]{1,2,0:T(8,128)} fusion(bf16[33,128,128]{2,0,1:T(8,128)(2,1)S(1)} %get-tuple-element.28, bf16[33,128,128]{2,1,0:T(8,128)(2,1)S(1)} %copy-done, bf16[33,128,128]{2,1,0:T(8,128)(2,1)S(1)} %get-tuple-element.41), kind=kOutput, calls=%fused_computation.49 | convolution fusion | flops 281149440 | bytes 7569408 | tf_op jit(solution)/shard_map/kjm,kml->kjl/dot_general | solution.py:50
  93.0 2.8 %fusion.13 = f32[33,256,128]{1,2,0:T(8,128)} fusion(bf16[33,128,128]{2,0,1:T(8,128)(2,1)S(1)} %get-tuple-element.27, bf16[33,128,128]{2,1,0:T(8,128)(2,1)S(1)} %copy-done, bf16[33,128,128]{2,1,0:T(8,128)(2,1)S(1)} %get-tuple-element.41), kind=kOutput, calls=%fused_computation.47 | convolution fusion | flops 281149440 | bytes 7569408 | tf_op jit(solution)/shard_map/kjm,kml->kjl/dot_general | solution.py:54
  97.6 1.9 copy.86
  100.8 1.2 copy.69
  102.0 3.2 %copy.38 = bf16[32,128,128]{2,0,1:T(8,128)(2,1)} copy(bf16[32,128,128]{1,0,2:T(8,128)(2,1)} %bitcast.129) | data formatting | bytes 2097152 | tf_op jit(solution)/shard_map/reshape | solution.py:84
  105.2 3.3 %convolution_convert_fusion = bf16[66,128,128]{2,0,1:T(8,128)(2,1)S(1)} fusion(bf16[32,128,128]{2,0,1:T(8,128)(2,1)} %copy.38, f32[33,32]{0,1:T(8,128)S(1)} %get-tuple-element.47, f32[33,32]{0,1:T(8,128)S(1)} %copy-done.18), kind=kOutput, calls=%fused_computation.25 | convolution fusion | flops 416319552 | bytes 3219712 | tf_op jit(solution)/shard_map/kn,nml->kml/dot_general | solution.py:66
  115.8 3.0 %fusion.7 = f32[33,256,128]{2,1,0:T(8,128)} fusion(f32[33,128,128]{1,2,0:T(8,128)S(1)} %get-tuple-element.24, f32[33,128,128]{1,2,0:T(8,128)S(1)} %get-tuple-element.23, f32[33,128,64]{1,2,0:T(8,128)S(1)} %get-tuple-element.32, f32[33,128,64]{1,2,0:T(8,128)S(1)} %get-tuple-element.31, f32[33,128,64]{1,2,0:T(8,128)S(1)} %get-tuple-element.30, ...), kind=kOutput, calls=%fused_computation.41 | convolution fusion | flops 284393472 | bytes 15138816 | tf_op jit(solution)/shard_map/kjm,kml->kjl/dot_general | solution.py:50
  118.7 2.9 %fusion.8 = f32[33,256,128]{2,1,0:T(8,128)} fusion(f32[33,128,128]{1,2,0:T(8,128)S(1)} %get-tuple-element.24, f32[33,128,128]{1,2,0:T(8,128)S(1)} %get-tuple-element.23, f32[33,128,64]{1,2,0:T(8,128)S(1)} %get-tuple-element.32, f32[33,128,64]{1,2,0:T(8,128)S(1)} %get-tuple-element.31, f32[33,128,64]{1,2,0:T(8,128)S(1)} %get-tuple-element.30, ...), kind=kOutput, calls=%fused_computation.42 | convolution fusion | flops 284393472 | bytes 15138816 | tf_op jit(solution)/shard_map/kjm,kml->kjl/dot_general | solution.py:54
  122.8 5.2 %fusion.2 = bf16[32,128,128]{2,0,1:T(8,128)(2,1)S(1)} fusion(f32[66,128,128]{2,1,0:T(8,128)S(1)} %pad_maximum_fusion, f32[32,33]{1,0:T(8,128)S(1)} %get-tuple-element.46, f32[32,33]{1,0:T(8,128)S(1)} %get-tuple-element.45), kind=kOutput, calls=%fused_computation.28 | convolution fusion | flops 415762496 | bytes 5382400 | tf_op jit(solution)/shard_map/nk,kml->nml/dot_general | solution.py:74
  128.0 1.5 copy.48
  130.5 4.5 %slice_subtract_fusion = (f32[33,128,128]{2,1,0:T(8,128)S(1)}, f32[33,128,128]{2,1,0:T(8,128)S(1)}) fusion(f32[33,256,128]{2,1,0:T(8,128)} %fusion.8, f32[33,256,128]{2,1,0:T(8,128)} %fusion.7), kind=kLoop, calls=%fused_computation.6 | loop fusion | flops 1081344 | bytes 12976128 | tf_op jit(solution)/shard_map/sub | solution.py:58
  135.0 2.6 %pad_maximum_fusion.1 = f32[66,128,128]{2,1,0:T(8,128)} fusion(f32[33,128,128]{2,1,0:T(8,128)S(1)} %get-tuple-element.22, f32[33,128,128]{2,1,0:T(8,128)S(1)} %get-tuple-element.21), kind=kLoop, calls=%fused_computation.3 | loop fusion | flops 1081344 | bytes 8650752 | tf_op jit(solution)/shard_map/concatenate | solution.py:73
  137.6 5.7 %copy.66 = f32[66,128,128]{1,0,2:T(8,128)} copy(f32[66,128,128]{2,1,0:T(8,128)} %pad_maximum_fusion.1) | data formatting | bytes 8650752 | tf_op jit(solution)/shard_map/concatenate | solution.py:73
  143.3 4.3 %fusion.59 = f32[32,128,128]{1,0,2:T(8,128)S(1)} fusion(f32[66,128,128]{1,0,2:T(8,128)} %copy.66, f32[32,33]{1,0:T(8,128)S(1)} %get-tuple-element.46, f32[32,33]{1,0:T(8,128)S(1)} %get-tuple-element.45), kind=kOutput, calls=%fused_computation.118 | convolution fusion | flops 415238208 | bytes 6430976 | tf_op jit(solution)/shard_map/nk,kml->nml/dot_general | solution.py:74
  147.6 1.6 reshape_reshape.4
  149.1 1.3 slice_reduce_fusion
  150.8 42.2 %all_to_all.10 = bf16[16,96,512]{2,1,0:T(8,128)(2,1)S(1)} all-to-all(bf16[16,96,512]{2,1,0:T(8,128)(2,1)S(1)} %pad_maximum_fusion.6), channel_id=1, replica_groups=mesh['seq'=8,'chan'=16,'dp'=2] {'seq','dp'}, dimensions={0} | all-to-all | bytes 3145728 | tf_op jit(solution)/shard_map/all_to_all | solution.py:152
  194.9 1.5 fusion.26
  196.3 2.0 %copy.55 = bf16[1,512,512]{2,1,0:T(8,128)(2,1)} copy(bf16[1,512,512]{1,2,0:T(8,128)(2,1)} %get-tuple-element.43) | data formatting | bytes 1048576
  201.5 1.3 copy.59
  (95 shorter events, 24.3 us)
Async XLA Ops:
  0.6 2.8 %copy-start.15 = (bf16[1,512,512]{2,1,0:T(8,128)(2,1)S(1)}, bf16[1,512,512]{2,1,0:T(8,128)(2,1)}, u32[]{:S(2)}) copy-start(bf16[1,512,512]{2,1,0:T(8,128)(2,1)} %param.7) | copy-start | bytes 1572868
  0.6 3.1 %copy-start.16 = (bf16[1,512,512]{2,1,0:T(8,128)(2,1)S(1)}, bf16[1,512,512]{2,1,0:T(8,128)(2,1)}, u32[]{:S(2)}) copy-start(bf16[1,512,512]{2,1,0:T(8,128)(2,1)} %param.8) | copy-start | bytes 1572868
  2.0 2.3 %copy-start.2 = (bf16[1,512,512]{1,2,0:T(8,128)(2,1)}, bf16[1,512,512]{1,2,0:T(8,128)(2,1)S(1)}, u32[]{:S(2)}) copy-start(bf16[1,512,512]{1,2,0:T(8,128)(2,1)S(1)} %copy.27) | copy-start | bytes 1572868
  3.5 0.9 copy-start.4
  3.7 1.5 copy-start.6
  3.9 1.3 copy-start.8
  4.3 0.8 copy-start.10
  4.4 1.0 copy-start.12
  4.4 1.6 copy-start.14
  39.3 37.8 %all-to-all-start = ((bf16[16,80,512]{2,1,0:T(8,128)(2,1)}), bf16[16,80,512]{2,1,0:T(8,128)(2,1)}, u32[]{:S(2)}, u32[]{:S(2)}) async-start(bf16[16,80,512]{2,1,0:T(8,128)(2,1)} %pad_maximum_fusion.7), calls=%async_computation | async-start | bytes 2621440 | tf_op jit(solution)/shard_map/all_to_all | solution.py:127
  44.9 40.8 %copy-start.17 = (f32[33,32]{0,1:T(8,128)}, f32[33,32]{0,1:T(8,128)S(1)}, u32[]{:S(2)}) copy-start(f32[33,32]{0,1:T(8,128)S(1)} %get-tuple-element.48) | copy-start | bytes 12676
  89.0 1.2 copy-start
  100.8 4.4 %copy-start.18 = (f32[33,32]{0,1:T(8,128)S(1)}, f32[33,32]{0,1:T(8,128)}, u32[]{:S(2)}) copy-start(f32[33,32]{0,1:T(8,128)} %copy-done.17) | copy-start | bytes 12676
  108.6 1.2 copy-start.1
  108.6 2.8 %slice-start.2 = ((s8[4325376]{0:T(1024)(128)(4,1)}), s8[4194304]{0:T(1024)(128)(4,1)S(1)}, s32[]{:S(2)}) async-start(s8[4325376]{0:T(1024)(128)(4,1)} %bitcast.120), calls=%async_computation.4 | async-start | bytes 8388608
  109.8 2.8 %slice-start = ((s8[4325376]{0:T(1024)(128)(4,1)}), s8[4194304]{0:T(1024)(128)(4,1)S(1)}, s32[]{:S(2)}) async-start(s8[4325376]{0:T(1024)(128)(4,1)} %bitcast.118), calls=%async_computation.2 | async-start | bytes 8388608
  109.8 2.8 %slice-start.3 = ((s8[4325376]{0:T(1024)(128)(4,1)}), s8[131072]{0:T(1024)(128)(4,1)S(1)}, s32[]{:S(2)}) async-start(s8[4325376]{0:T(1024)(128)(4,1)} %bitcast.120), calls=%async_computation.5 | async-start | bytes 262144
  110.6 2.0 slice-start.1
  112.6 0.6 copy-start.19
  193.0 1.0 copy-start.3
  193.0 1.2 copy-start.5
  193.0 1.4 copy-start.7
  193.0 1.5 copy-start.9
  193.0 1.7 copy-start.11
  193.0 1.8 copy-start.13
  193.1 1.8 copy-start.20
